TPU v7x, 128 devices: a whole 4x4x4 slice. The times are simulated.
128 devices in a mesh: req: 4 (over y), head: 32 (over x, z, core).
Axes of the slice: x: 4, y: 4, z: 4, core: 2. Of those that a mesh axis runs over, the one named last changes fastest.
Arguments:
- hidden_in: bfloat16 [8192, 2048], P(('req', 'head')), may hold values from -6 to 6
- queries: bfloat16 [8192, 2048], P(('req', 'head')), may hold values from -160 to 160
- keys_values: bfloat16 [8192, 1024], P(('req', 'head')), may hold values from -10 to 10
- request_of_row: int32 [8192], P('req'), may hold values from 0 to 7, as said below
- page_route: int32 [4, 32, 4], P('req', 'head'), may hold values from 0 to 3, each once within a row
- expert_ids: int32 [8192, 6], P(('req', 'head')), may hold values from 0 to 31, all different within a row; in each aligned block of 64 rows (0 to 63, 64 to 127, ...) at most 14 rows name the same one
- expert_weights: float32 [8192, 6], P(('req', 'head')), may hold values from 0.05 to 0.5
- norm_gain: float32 [2048], replicated, may hold values from 0.25 to 1.75
- shared_gate_up: bfloat16 [2048, 2, 1408], replicated, may hold values from -0.125 to 0.125
- shared_down: bfloat16 [1408, 2048], replicated, may hold values from -0.15625 to 0.15625
- expert_gate_up: bfloat16 [32, 2, 1408, 2048], P('head', None, 'req'), may hold values from -0.125 to 0.125
- expert_down: bfloat16 [32, 1408, 2048], P('head', 'req'), may hold values from -0.15625 to 0.15625
Outputs:
- layer_out: bfloat16 [8192, 2048], P(('req', 'head'))
Inputs may be any that keep to these rules, and one draw needn't show every extreme that they name: `request_of_row`: each group of 2048 rows g holds two requests, ids 2 g then 2 g + 1, each a whole number of pages of 16 rows and at least 128 rows long. `page_route`: for every device, the groups receiving its pages form a permutation of all groups. `expert_ids`: each row names 6 different experts; among the rows of one device no expert is named more than 14 times, and some device names some expert exactly 14 times.
All inputs are finite; a program needn't handle non-finite values.
Results may differ from a plain program's by a relative error of at most 0.006.
Values may be sent and summed in bfloat16 or wider, within the bound.
No kernel may reach another device: no remote copies, remote signals or barrier semaphores. Data moves between devices by JAX's collectives and lax.ppermute only.
A program may use at most 192 MiB of HBM per device.

v0:
```python
import jax
import jax.numpy as jnp
from jax import lax
from jax.sharding import PartitionSpec as P

QUERY_HEADS = 16
KEY_VALUE_HEADS = 4
HEAD_SIZE = 128
EXPERTS = 32
TOP = 6
CAP = 14
negative_large = -1e30


def silu_mul(gate_value, upward):
    return gate_value / (1.0 + jnp.exp(-gate_value)) * upward


def body(
    hidden_in,
    queries,
    keys_values,
    request_of_row,
    page_route,
    expert_ids,
    expert_weights,
    norm_gain,
    shared_gate_up,
    shared_down,
    expert_gate_up,
    expert_down,
):
    groups = lax.axis_size("req")
    columns = lax.axis_size("head")
    token_rows = hidden_in.shape[0]
    model_width = hidden_in.shape[1]
    page_rows = token_rows // groups
    group_ids = jnp.arange(groups, dtype=jnp.int32)
    page_dest = page_route.reshape(groups)
    matches = (page_dest[None, :] == group_ids[:, None]).astype(jnp.int32)
    dest_order = jnp.sum(matches * group_ids[None, :], axis=1)

    def by_dest(array_in):
        return jnp.take(array_in.reshape(groups, page_rows, array_in.shape[1]), dest_order, axis=0)

    widths = (hidden_in.shape[1], queries.shape[1], keys_values.shape[1])
    packed = jnp.concatenate((hidden_in, queries, keys_values), axis=1)
    moved = lax.all_to_all(by_dest(packed), "req", split_axis=0, concat_axis=0, tiled=True)
    moved = moved.reshape(token_rows, sum(widths))
    resid = moved[:, : widths[0]]
    rows_of_queries = moved[:, widths[0] : widths[0] + widths[1]]
    key_value_rows = moved[:, widths[0] + widths[1] :]
    group_fraction = QUERY_HEADS // KEY_VALUE_HEADS
    key_value_width = KEY_VALUE_HEADS * HEAD_SIZE
    score_scale = HEAD_SIZE ** (-0.5)
    query_start = lax.axis_index("head") * token_rows
    segment_query = lax.dynamic_slice_in_dim(request_of_row, query_start, token_rows)
    position_query = query_start + jnp.arange(token_rows, dtype=jnp.int32)
    query_fourfold = rows_of_queries.reshape(token_rows, KEY_VALUE_HEADS, group_fraction, HEAD_SIZE)
    start_state = (
        jnp.full((KEY_VALUE_HEADS, group_fraction, token_rows), negative_large, jnp.float32),
        jnp.zeros((KEY_VALUE_HEADS, group_fraction, token_rows), jnp.float32),
        jnp.zeros((KEY_VALUE_HEADS, group_fraction, token_rows, HEAD_SIZE), jnp.float32),
    )
    kv_piece = lax.all_gather(key_value_rows, "head", axis=0, tiled=True)
    piece_rows = kv_piece.shape[0]
    rows_per_block = 512

    def one_block(block_index, carried_block):
        offset = block_index * rows_per_block
        current_block = lax.dynamic_slice_in_dim(kv_piece, offset, rows_per_block)
        block_keys = current_block[:, :key_value_width].reshape(
            rows_per_block, KEY_VALUE_HEADS, HEAD_SIZE
        )
        block_values = current_block[:, key_value_width:].reshape(
            rows_per_block, KEY_VALUE_HEADS, HEAD_SIZE
        )
        segment_key = lax.dynamic_slice_in_dim(request_of_row, offset, rows_per_block)
        position_key = offset + jnp.arange(rows_per_block, dtype=jnp.int32)
        allowed = (segment_query[:, None] == segment_key[None, :]) & (
            position_key[None, :] <= position_query[:, None]
        )
        running_max, running_sum, accumulated = carried_block
        score = (
            jnp.einsum(
                "tgqd,sgd->gqts", query_fourfold, block_keys, preferred_element_type=jnp.float32
            )
            * score_scale
        )
        masked = jnp.where(allowed, score, negative_large)
        new_max = jnp.maximum(running_max, jnp.max(masked, axis=-1))
        weights = jnp.where(allowed, jnp.exp(masked - new_max[..., None]), 0.0)
        factor = jnp.exp(running_max - new_max)
        running_sum = running_sum * factor + jnp.sum(weights, axis=-1)
        accumulated = accumulated * factor[..., None] + jnp.einsum(
            "gqts,sgd->gqtd",
            weights.astype(jnp.bfloat16),
            block_values,
            preferred_element_type=jnp.float32,
        )
        return (new_max, running_sum, accumulated)

    running_max, running_sum, accumulated = lax.fori_loop(
        0, piece_rows // rows_per_block, one_block, start_state
    )
    context = jnp.transpose(accumulated / running_sum[..., None], (2, 0, 1, 3)).reshape(
        token_rows, QUERY_HEADS * HEAD_SIZE
    )
    mixed_rows = resid.astype(jnp.float32) + context
    mean_square = jnp.mean(mixed_rows * mixed_rows, axis=1, keepdims=True)
    normed = (mixed_rows * lax.rsqrt(mean_square + 1e-06) * norm_gain).astype(jnp.bfloat16)
    pair_expert = expert_ids.reshape(-1)
    hit_table = (pair_expert[:, None] == jnp.arange(EXPERTS, dtype=jnp.int32)[None, :]).astype(
        jnp.int32
    )
    ranks = jnp.sum((jnp.cumsum(hit_table, axis=0) - 1) * hit_table, axis=1)
    slot_of = pair_expert * CAP + ranks
    slots_all = EXPERTS * CAP
    placing = jnp.arange(slots_all, dtype=jnp.int32)[:, None] == slot_of[None, :]
    placing = jnp.any(placing.reshape(slots_all, token_rows, TOP), axis=2).astype(jnp.bfloat16)
    outgoing = jnp.dot(placing, normed, preferred_element_type=jnp.float32).astype(jnp.bfloat16)
    local_experts = expert_gate_up.shape[0]
    outgoing = outgoing.reshape(columns, local_experts * CAP, model_width)
    shared_both = jnp.dot(
        normed, shared_gate_up.reshape(model_width, -1), preferred_element_type=jnp.float32
    ).reshape(token_rows, 2, -1)
    shared_hidden = silu_mul(shared_both[:, 0], shared_both[:, 1]).astype(jnp.bfloat16)
    shared_out = jnp.dot(shared_hidden, shared_down, preferred_element_type=jnp.float32)
    at_expert = lax.all_to_all(outgoing, "head", split_axis=0, concat_axis=0, tiled=True)
    gathered = lax.all_gather(at_expert, "req", axis=0, tiled=True)
    expert_rows = gathered.reshape(-1, model_width)
    both_parts = jnp.einsum(
        "nd,kfd->nkf", expert_rows, expert_gate_up[0], preferred_element_type=jnp.float32
    )
    hidden = silu_mul(both_parts[:, 0], both_parts[:, 1]).astype(jnp.bfloat16)
    part_out = jnp.dot(hidden, expert_down[0], preferred_element_type=jnp.float32).astype(
        jnp.bfloat16
    )
    part_sum = lax.psum_scatter(part_out, "req", scatter_dimension=0, tiled=True)
    returned = lax.all_to_all(
        part_sum.reshape(columns, local_experts * CAP, model_width),
        "head",
        split_axis=0,
        concat_axis=0,
        tiled=True,
    )
    summed = returned.reshape(slots_all, model_width)
    pair_rows = jnp.take(summed, slot_of, axis=0).reshape(token_rows, TOP, model_width)
    routed = jnp.sum(pair_rows.astype(jnp.float32) * expert_weights[:, :, None], axis=1)
    return (mixed_rows + shared_out + routed).astype(jnp.bfloat16)


def solution(mesh):
    return jax.shard_map(
        body,
        mesh=mesh,
        in_specs=(
            P(("req", "head"), None),
            P(("req", "head"), None),
            P(("req", "head"), None),
            P("req"),
            P("req", "head", None),
            P(("req", "head"), None),
            P(("req", "head"), None),
            P(),
            P(),
            P(),
            P("head", None, "req", None),
            P("head", "req", None),
        ),
        out_specs=P(("req", "head"), None),
        check_vma=False,
    )
```

profile of v0, /device:TPU:1, one launch (start us, length us, event | category | flops | bytes accessed | tf_op | source)
XLA Modules:
  0.0 419.0 jit_solution(10034668112566596704)
XLA Ops:
  7.5 2.0 pad_maximum_fusion
  11.3 14.8 %all_to_all.15 = bf16[4,16,5120]{2,1,0:T(8,128)(2,1)S(1)} all-to-all(bf16[4,16,5120]{2,1,0:T(8,128)(2,1)S(1)} %broadcast_select_fusion), channel_id=1, replica_groups=mesh['req'=4,'head'=32] {'req'}, dimensions={0} | all-to-all | bytes 1310720 | tf_op jit(solution)/shard_map/all_to_all | solution.py:48
  32.5 2.6 reduce-window.6
  49.9 25.2 %all-gather.3.cloned.1.call-done = bf16[2048,1024]{1,0:T(8,128)(2,1)} async-done(((bf16[64,1024]{1,0:T(8,128)(2,1)}), bf16[2048,1024]{1,0:T(8,128)(2,1)}) %all-gather.3.cloned.1.call-update) | async-done | bytes 4194320 | tf_op jit(solution)/shard_map/all_gather | solution.py:65
  75.0 43.0 %while.18 = (s32[]{:T(128)}, f32[4,4,64]{2,1,0:T(4,128)S(1)}, f32[4,4,64]{2,1,0:T(4,128)S(1)}, f32[4,4,64,128]{3,2,1,0:T(8,128)}, s32[64]{0:T(128)}, /*index=5*/...) while((s32[]{:T(128)}, f32[4,4,64]{2,1,0:T(4,128)S(1)}, ...), condition=%wide.region_4.5_spmd.clone, body=%wide.region_1.4_spmd.clone.sunk | while | flops 275748416 | bytes 19344444 | solution.py:103
  76.5 2.1 fusion.59
  78.6 2.1 copy.86
  87.3 2.1 fusion.59
  89.3 2.1 copy.86
  98.0 2.1 fusion.59
  100.1 2.1 copy.86
  108.7 2.1 fusion.59
  110.8 2.1 copy.86
  126.5 3.6 reshape.171
  130.2 33.4 %all_to_all.16 = bf16[32,14,2048]{2,1,0:T(8,128)(2,1)S(1)} all-to-all(bf16[32,14,2048]{2,1,0:T(8,128)(2,1)} %reshape.171), channel_id=1, replica_groups=mesh['req'=4,'head'=32] {'head'}, dimensions={0} | all-to-all | bytes 3670016 | tf_op jit(solution)/shard_map/all_to_all | solution.py:129
  163.6 2.3 copy.68
  166.1 71.6 %all-gather.5.cloned.1.call-done = bf16[128,14,2048]{2,0,1:T(8,128)(2,1)} async-done(((bf16[32,14,2048]{2,0,1:T(8,128)(2,1)}), bf16[128,14,2048]{2,0,1:T(8,128)(2,1)}) %all-gather.5.cloned.1.call-update) | async-done | bytes 7340048 | tf_op jit(solution)/shard_map/all_gather | solution.py:130
  237.8 10.4 %copy.69 = bf16[128,14,2048]{2,1,0:T(8,128)(2,1)} copy(bf16[128,14,2048]{2,0,1:T(8,128)(2,1)} %all-gather.5.cloned.1.call-done) | data formatting | bytes 14680064 | tf_op jit(solution)/shard_map/all_gather | solution.py:130
  248.2 10.5 %reshape.196 = bf16[1792,2048,1]{1,0,2:T(8,128)(2,1)} reshape(bf16[128,14,2048]{2,1,0:T(8,128)(2,1)} %copy.69) | data formatting | bytes 14680064 | tf_op jit(solution)/shard_map/reshape | solution.py:131
  258.7 8.6 %fusion.14 = f32[1792,2,352]{0,2,1:T(8,128)S(1)} fusion(bf16[1792,2048,1]{1,0,2:T(8,128)(2,1)} %reshape.196, bf16[1,2,352,2048]{3,2,1,0:T(8,128)(2,1)S(1)} %copy-done), kind=kOutput, calls=%fused_computation.28 | convolution fusion | flops 5167382528 | bytes 15269888 | tf_op jit(solution)/shard_map/nd,kfd->nkf/dot_general | solution.py:132
  267.3 6.2 %convolution_convert_fusion = bf16[1792,2048]{1,0:T(8,128)(2,1)} fusion(bf16[1,352,2048]{2,1,0:T(8,128)(2,1)S(1)} %copy-done.15, f32[1792,2,352]{0,2,1:T(8,128)S(1)} %fusion.14), kind=kOutput, calls=%fused_computation.25 | convolution fusion | flops 2590515200 | bytes 13828096 | tf_op jit(solution)/shard_map/dot_general | solution.py:136
  273.5 73.6 %reduce-scatter.2.cloned.1.call-done = bf16[448,2048]{1,0:T(8,128)(2,1)} async-done(((bf16[1792,2048]{1,0:T(8,128)(2,1)}), bf16[448,2048]{1,0:T(8,128)(2,1)}) %reduce-scatter.2.cloned.1.call-update) | async-done | bytes 1835024 | tf_op jit(solution)/shard_map/reduce_scatter | solution.py:139
  347.1 3.6 reshape.173
  350.7 7.9 %all-to-all-start.2 = ((bf16[32,14,2048]{2,1,0:T(8,128)(2,1)}), bf16[32,14,2048]{2,1,0:T(8,128)(2,1)}, u32[]{:S(2)}, u32[]{:S(2)}) async-start(bf16[32,14,2048]{2,1,0:T(8,128)(2,1)} %reshape.173), calls=%async_computation.3 | async-start | bytes 4194304 | tf_op jit(solution)/shard_map/all_to_all | solution.py:140
  359.2 11.3 %copy.82 = bf16[256,8,2,1408]{3,1,2,0:T(8,128)(2,1)} copy(bf16[256,8,2,1408]{3,2,1,0:T(2,128)(2,1)} %bitcast.103) | data formatting | bytes 23068672
  370.4 15.2 %copy.62 = bf16[2816,2048]{1,0:T(8,128)(2,1)} copy(bf16[2816,2048]{0,1:T(8,128)(2,1)} %bitcast.101) | data formatting | bytes 23068672 | tf_op jit(solution)/shard_map/dot_general | solution.py:124
  385.7 8.7 %fusion.25 = f32[64,2,1408]{2,0,1:T(8,128)} fusion(bf16[2,1408,2048]{2,1,0:T(8,128)(2,1)} %bitcast.100, bf16[64,2048]{1,0:T(8,128)(2,1)S(1)} %copy-done.6), kind=kOutput, calls=%fused_computation.49 | convolution fusion | flops 738197504 | bytes 12517376 | tf_op jit(solution)/shard_map/dot_general | solution.py:124
  394.4 2.5 reshape.174
  396.9 3.1 gather_fusion.1
  400.1 3.7 gather.12
  403.8 4.2 multiply_reduce_fusion
  407.9 4.5 %fusion.18 = bf16[64,2048]{1,0:T(8,128)(2,1)} fusion(f32[64,2048]{1,0:T(8,128)S(1)} %multiply_reduce_fusion, bf16[1408,2048]{1,0:T(8,128)(2,1)} %param.23, f32[64,2,1408]{2,0,1:T(8,128)S(1)} %copy-done.4, f32[64,2048]{1,0:T(8,128)S(1)} %reshape.167, bf16[64,5120]{1,0:T(8,128)(2,1)} %bitcast.108), kind=kOutput, calls=%fused_computation.34 | convolution fusion | flops 370204672 | bytes 8060928 | tf_op jit(solution)/shard_map/dot_general | solution.py:128
  (140 shorter events, 59.2 us)
Async XLA Ops:
  6.5 252.2 %copy-start = (bf16[1,2,352,2048]{3,2,1,0:T(8,128)(2,1)S(1)}, bf16[1,2,352,2048]{3,2,1,0:T(8,128)(2,1)}, u32[]{:S(2)}) copy-start(bf16[1,2,352,2048]{3,2,1,0:T(8,128)(2,1)} %param.24) | copy-start | bytes 8650756
  6.5 68.5 %all-gather.3.cloned.1.call-start = ((), (), s32[]{:S(2)}) async-start(), calls=%async_computation.4 | async-start | bytes 4325376 | tf_op jit(solution)/shard_map/all_gather | solution.py:65
  26.1 48.9 %copy-start.3 = (bf16[4,16,5120]{2,1,0:T(8,128)(2,1)}, bf16[4,16,5120]{2,1,0:T(8,128)(2,1)S(1)}, u32[]{:S(2)}) copy-start(bf16[4,16,5120]{2,1,0:T(8,128)(2,1)S(1)} %all_to_all.15) | copy-start | bytes 1966084
  26.8 210.9 %all-gather.5.cloned.1.call-start = ((), (), s32[]{:S(2)}) async-start(), calls=%async_computation.5 | async-start | bytes 9175040 | tf_op jit(solution)/shard_map/all_gather | solution.py:130
  81.7 2.5 copy-start.2
  81.7 2.5 copy-start.7
  85.0 0.8 copy-start.8
  92.4 2.5 copy-start.2
  92.4 2.5 copy-start.7
  95.7 0.8 copy-start.8
  103.2 2.5 copy-start.2
  103.2 2.5 copy-start.7
  106.5 0.8 copy-start.8
  113.9 2.5 copy-start.2
  113.9 2.5 copy-start.7
  117.2 0.8 copy-start.8
  118.0 4.8 %copy-start.12 = (f32[2048]{0:T(1024)S(1)}, f32[2048]{0:T(1024)}, u32[]{:S(2)}) copy-start(f32[2048]{0:T(1024)} %param.21) | copy-start | bytes 24580
  119.3 5.3 %copy-start.9 = (pred[448,64]{0,1:T(8,128)(4,1)S(1)}, pred[448,64]{0,1:T(8,128)(4,1)}, u32[]{:S(2)}) copy-start(pred[448,64]{0,1:T(8,128)(4,1)} %fusion.22) | copy-start | bytes 86020
  123.9 0.7 copy-start.5
  165.9 181.2 %reduce-scatter.2.cloned.1.call-start = ((), (), s32[]{:S(2)}) async-start(), calls=%async_computation.6 | async-start | bytes 9175040 | tf_op jit(solution)/shard_map/reduce_scatter | solution.py:139
  258.7 8.6 %copy-start.15 = (bf16[1,352,2048]{2,1,0:T(8,128)(2,1)S(1)}, bf16[1,352,2048]{2,1,0:T(8,128)(2,1)}, u32[]{:S(2)}) copy-start(bf16[1,352,2048]{2,1,0:T(8,128)(2,1)} %param.25) | copy-start | bytes 4325380
  350.7 8.0 %copy-start.10 = (s32[64,6]{0,1:T(8,128)S(1)}, s32[64,6]{0,1:T(8,128)}, u32[]{:S(2)}) copy-start(s32[64,6]{0,1:T(8,128)} %param.19) | copy-start | bytes 4612
  350.7 8.2 %copy-start.13 = (f32[64,6]{0,1:T(8,128)S(1)}, f32[64,6]{0,1:T(8,128)}, u32[]{:S(2)}) copy-start(f32[64,6]{0,1:T(8,128)} %param.20) | copy-start | bytes 4612
  350.7 8.3 %copy-start.14 = (pred[64,6]{0,1:T(8,128)(4,1)S(1)}, pred[64,6]{0,1:T(8,128)(4,1)}, u32[]{:S(2)}) copy-start(pred[64,6]{0,1:T(8,128)(4,1)} %get-tuple-element.260) | copy-start | bytes 1156
  350.7 43.7 %all-to-all-start.2 = ((bf16[32,14,2048]{2,1,0:T(8,128)(2,1)}), bf16[32,14,2048]{2,1,0:T(8,128)(2,1)}, u32[]{:S(2)}, u32[]{:S(2)}) async-start(bf16[32,14,2048]{2,1,0:T(8,128)(2,1)} %reshape.173), calls=%async_computation.3 | async-start | bytes 4194304 | tf_op jit(solution)/shard_map/all_to_all | solution.py:140
  370.4 15.2 %copy-start.11 = (s32[384]{0:T(512)S(1)}, s32[384]{0:T(512)}, u32[]{:S(2)}) copy-start(s32[384]{0:T(512)} %fusion.30) | copy-start | bytes 4612
  370.4 15.2 %copy-start.6 = (bf16[64,2048]{1,0:T(8,128)(2,1)S(1)}, bf16[64,2048]{1,0:T(8,128)(2,1)}, u32[]{:S(2)}) copy-start(bf16[64,2048]{1,0:T(8,128)(2,1)} %copy-done.5) | copy-start | bytes 786436
  403.8 4.2 copy-start.4
  403.8 8.7 %copy-start.1 = (bf16[1,2,352,2048]{3,2,1,0:T(8,128)(2,1)S(1)}, bf16[1,2,352,2048]{3,2,1,0:T(8,128)(2,1)}, u32[]{:S(2)}) copy-start(bf16[1,2,352,2048]{3,2,1,0:T(8,128)(2,1)} %param.24) | copy-start | bytes 8650756
Sparse Core Ops, SparseCore 0:
  27.0 48.0 all-gather.2
  166.0 71.7 all-gather.4
  273.6 73.4 reduce-scatter.1
where the time goes:
time: 422 us; the launch traced here: 419 us
  waiting for transfers between devices  170 us (40%)
  local copies, waits for them, and re-layouts  113 us (27%)
  blocking collectives  48.3 us (11%)
  matrix products  40.1 us (10%)
  other arithmetic  25 us (6%)
  between operations  13.3 us (3%)
  starting transfers between devices  8.2 us (2%)
    reduce_scatter x1, waiting for transfers between devices, body(): lax.psum_scatter(part_out, 'req', scatter_dimension=0, tiled=True)  73.6 us
    all_gather x1, waiting for transfers between devices, body(): gathered = lax.all_gather(at_expert, 'req', axis=0, tiled=True)  71.6 us
    all_to_all x1, blocking collectives, body(): lax.all_to_all(outgoing, 'head', split_axis=0, concat_axis=0, tiled=True)  33.4 us
    all_gather x1, waiting for transfers between devices, body(): kv_piece = lax.all_gather(key_value_rows, 'head', axis=0, tiled=True)  25.2 us
    while x36, local copies, waits for them, and re-layouts  15.5 us
    unnamed x30, local copies, waits for them, and re-layouts  15.2 us
    dot_general x1, local copies, waits for them, and re-layouts, body(): jnp.dot(normed, shared_gate_up.reshape(model_width, -1), preferred_elemen...  15.2 us
    all_to_all x1, blocking collectives, body(): lax.all_to_all(by_dest(packed), 'req', split_axis=0, concat_axis=0, tiled...  14.8 us
  transfers between devices with their start and end apart: 4, of which 3 were waited for; matrix products, arithmetic and copies ran while one was open for 14% of the time, Pallas kernels for 0%

commit v1 on v0

--- a/solution.py
+++ b/solution.py
@@ -10,6 +10,35 @@
 TOP = 6
 CAP = 14
 negative_large = -1e30
+
+
+def quotas_pass(x_local, dim_i):
+    parts_out, odd, view_out = (
+        jax.lax.axis_size("req"),
+        jax.lax.axis_index("req"),
+        x_local.shape[dim_i],
+    )
+    found_now = jnp.zeros(
+        [jj * parts_out if ix == dim_i else jj for ix, jj in enumerate(x_local.shape)],
+        x_local.dtype,
+    )
+    row_out = x_now = x_local
+    v1 = lax.dynamic_update_slice_in_dim(found_now, x_local, odd * view_out, axis=dim_i)
+    for s in range(1, parts_out // 2 + 1):
+        row_out = jax.lax.ppermute(
+            row_out, "req", [(ix, (ix + 1) % parts_out) for ix in range(parts_out)]
+        )
+        v1 = lax.dynamic_update_slice_in_dim(
+            v1, row_out, (odd - s) % parts_out * view_out, axis=dim_i
+        )
+        if 2 * s < parts_out:
+            x_now = jax.lax.ppermute(
+                x_now, "req", [(ix, (ix - 1) % parts_out) for ix in range(parts_out)]
+            )
+            v1 = lax.dynamic_update_slice_in_dim(
+                v1, x_now, (odd + s) % parts_out * view_out, axis=dim_i
+            )
+    return v1
 
 
 def silu_mul(gate_value, upward):
@@ -127,7 +156,7 @@
     shared_hidden = silu_mul(shared_both[:, 0], shared_both[:, 1]).astype(jnp.bfloat16)
     shared_out = jnp.dot(shared_hidden, shared_down, preferred_element_type=jnp.float32)
     at_expert = lax.all_to_all(outgoing, "head", split_axis=0, concat_axis=0, tiled=True)
-    gathered = lax.all_gather(at_expert, "req", axis=0, tiled=True)
+    gathered = quotas_pass(at_expert, 0)
     expert_rows = gathered.reshape(-1, model_width)
     both_parts = jnp.einsum(
         "nd,kfd->nkf", expert_rows, expert_gate_up[0], preferred_element_type=jnp.float32

time: 422 us -> 444 us (1.052)
  matrix products: 40.1 us -> 54.9 us
  waiting for transfers between devices: 170 us -> 163 us
  other arithmetic: 25 us -> 31.7 us
  local copies, waits for them, and re-layouts: 113 us -> 119 us
    all_gather x1 -> x0, waiting for transfers between devices: 71.6 us -> none  [body(): gathered = lax.all_gather(at_expert, 'req', axis=0, tiled=True)]
    ppermute x0 -> x3, waiting for transfers between devices: none -> 69 us  [the longest x2 69 us: quotas_pass(): jax.lax.ppermute(row_out, 'req', [(ix, (ix + 1) % parts_out) for ix in ra...]
    dynamic_update_slice x0 -> x4, local copies, waits for them, and re-layouts: none -> 13 us  [the longest x2 7.7 us: quotas_pass(): lax.dynamic_update_slice_in_dim(v1, row_out, (odd - s) % parts_out * view...]
    all_gather x1 -> x0, local copies, waits for them, and re-layouts: 10.4 us -> none  [body(): gathered = lax.all_gather(at_expert, 'req', axis=0, tiled=True)]
    dot_general x4, matrix products: 3.33 us -> 13.4 us  [one_block(): jnp.einsum('gqts,sgd->gqtd', weights.astype(jnp.bfloat16), block_values,...]
    reduce_sum x4, other arithmetic: 2.83 us -> 9.06 us  [one_block(): running_sum = running_sum * factor + jnp.sum(weights, axis=-1)]
    dot_general x4, matrix products: 6.83 us -> 11.5 us  [one_block(): jnp.einsum('tgqd,sgd->gqts', query_fourfold, block_keys, preferred_elemen...]
    reduce_scatter x1, waiting for transfers between devices: 73.6 us -> 69.1 us  [body(): lax.psum_scatter(part_out, 'req', scatter_dimension=0, tiled=True)]
  transfers between devices with their start and end apart: 4 -> 6, of which waited for: 3 -> 4; matrix products, arithmetic and copies ran while one was open for 14% -> 16% of each run, Pallas kernels for 0% -> 0%
where the time goes in v1:
time: 444 us; the launch traced here: 441 us
  waiting for transfers between devices  163 us (37%)
  local copies, waits for them, and re-layouts  119 us (27%)
  matrix products  54.9 us (12%)
  blocking collectives  48.3 us (11%)
  other arithmetic  31.7 us (7%)
  between operations  13.6 us (3%)
  starting transfers between devices  10.7 us (2%)
    reduce_scatter x1, waiting for transfers between devices, body(): lax.psum_scatter(part_out, 'req', scatter_dimension=0, tiled=True)  69.1 us
    ppermute x2, waiting for transfers between devices, quotas_pass(): jax.lax.ppermute(row_out, 'req', [(ix, (ix + 1) % parts_out) for ix in ra...  69 us
    all_to_all x1, blocking collectives, body(): lax.all_to_all(outgoing, 'head', split_axis=0, concat_axis=0, tiled=True)  33.4 us
    all_gather x1, waiting for transfers between devices, body(): kv_piece = lax.all_gather(key_value_rows, 'head', axis=0, tiled=True)  25 us
    unnamed x34, local copies, waits for them, and re-layouts  16.6 us
    dot_general x1, local copies, waits for them, and re-layouts, body(): jnp.dot(normed, shared_gate_up.reshape(model_width, -1), preferred_elemen...  15.2 us
    all_to_all x1, blocking collectives, body(): lax.all_to_all(by_dest(packed), 'req', split_axis=0, concat_axis=0, tiled...  14.8 us
    dot_general x4, matrix products, one_block(): jnp.einsum('gqts,sgd->gqtd', weights.astype(jnp.bfloat16), block_values,...  13.4 us
  transfers between devices with their start and end apart: 6, of which 4 were waited for; matrix products, arithmetic and copies ran while one was open for 16% of the time, Pallas kernels for 0%

profile of v1, /device:TPU:1, one launch (start us, length us, event | category | flops | bytes accessed | tf_op | source)
XLA Modules:
  0.0 440.8 jit_solution(16055116626383563355)
XLA Ops:
  11.3 14.8 %all_to_all.15 = bf16[4,16,5120]{2,1,0:T(8,128)(2,1)S(1)} all-to-all(bf16[4,16,5120]{2,1,0:T(8,128)(2,1)S(1)} %broadcast_select_fusion), channel_id=1, replica_groups=mesh['req'=4,'head'=32] {'req'}, dimensions={0} | all-to-all | bytes 1310720 | tf_op jit(solution)/shard_map/all_to_all | solution.py:77
  50.1 25.0 %all-gather.2.cloned.1.call-done = bf16[2048,1024]{1,0:T(8,128)(2,1)} async-done(((bf16[64,1024]{1,0:T(8,128)(2,1)}), bf16[2048,1024]{1,0:T(8,128)(2,1)}) %all-gather.2.cloned.1.call-update) | async-done | bytes 4194320 | tf_op jit(solution)/shard_map/all_gather | solution.py:94
  75.0 61.0 %while.18 = (s32[]{:T(128)}, f32[4,4,64]{2,1,0:T(4,128)S(1)}, f32[4,4,64]{2,1,0:T(4,128)S(1)}, f32[4,4,64,128]{3,2,1,0:T(8,128)}, s32[64]{0:T(128)}, /*index=5*/...) while((s32[]{:T(128)}, f32[4,4,64]{2,1,0:T(4,128)S(1)}, ...), condition=%wide.region_4.5_spmd.clone, body=%wide.region_1.4_spmd.clone.sunk | while | flops 275748416 | bytes 13052895 | solution.py:132
  80.7 2.9 fusion.60
  86.9 3.2 convolution_add_fusion.3
  95.8 2.9 fusion.60
  102.0 3.4 convolution_add_fusion.3
  111.1 2.9 fusion.60
  117.3 3.4 convolution_add_fusion.3
  126.4 2.9 fusion.60
  132.6 3.4 convolution_add_fusion.3
  144.5 3.6 reshape.171
  148.1 33.4 %all_to_all.16 = bf16[32,14,2048]{2,1,0:T(8,128)(2,1)S(1)} all-to-all(bf16[32,14,2048]{2,1,0:T(8,128)(2,1)} %reshape.171), channel_id=1, replica_groups=mesh['req'=4,'head'=32] {'head'}, dimensions={0} | all-to-all | bytes 3670016 | tf_op jit(solution)/shard_map/all_to_all | solution.py:158
  187.9 40.3 %collective-permute-done = bf16[32,14,2048]{2,0,1:T(8,128)(2,1)} collective-permute-done((bf16[32,14,2048]{2,0,1:T(8,128)(2,1)}, bf16[32,14,2048]{2,0,1:T(8,128)(2,1)}, u32[]{:S(2)}, u32[]{:S(2)}) %collective-permute-start) | collective-permute-done | bytes 1835040 | tf_op jit(solution)/shard_map/ppermute | solution.py:28
  228.2 4.3 broadcast_in_dim.89
  234.0 3.9 copy_dynamic-update-slice_fusion.2
  237.8 3.8 copy_dynamic-update-slice_fusion.1
  241.6 28.7 %collective-permute-done.2 = bf16[32,14,2048]{2,0,1:T(8,128)(2,1)} collective-permute-done((bf16[32,14,2048]{2,0,1:T(8,128)(2,1)}, bf16[32,14,2048]{2,0,1:T(8,128)(2,1)}, u32[]{:S(2)}, u32[]{:S(2)}) %collective-permute-start.2) | collective-permute-done | bytes 1835040 | tf_op jit(solution)/shard_map/ppermute | solution.py:28
  270.3 3.8 copy_dynamic-update-slice_fusion
  274.2 10.5 %reshape.196 = bf16[1792,2048,1]{1,0,2:T(8,128)(2,1)} reshape(bf16[128,14,2048]{2,1,0:T(8,128)(2,1)} %copy_dynamic-update-slice_fusion) | data formatting | bytes 14680064 | tf_op jit(solution)/shard_map/reshape | solution.py:160
  284.7 8.6 %fusion.14 = f32[1792,2,352]{0,2,1:T(8,128)S(1)} fusion(bf16[1792,2048,1]{1,0,2:T(8,128)(2,1)} %reshape.196, bf16[1,2,352,2048]{3,2,1,0:T(8,128)(2,1)S(1)} %copy-done), kind=kOutput, calls=%fused_computation.28 | convolution fusion | flops 5167382528 | bytes 15269888 | tf_op jit(solution)/shard_map/nd,kfd->nkf/dot_general | solution.py:161
  293.3 6.2 %convolution_convert_fusion = bf16[1792,2048]{1,0:T(8,128)(2,1)} fusion(bf16[1,352,2048]{2,1,0:T(8,128)(2,1)S(1)} %copy-done.14, f32[1792,2,352]{0,2,1:T(8,128)S(1)} %fusion.14), kind=kOutput, calls=%fused_computation.25 | convolution fusion | flops 2590515200 | bytes 13828096 | tf_op jit(solution)/shard_map/dot_general | solution.py:165
  299.5 69.1 %reduce-scatter.2.cloned.1.call-done = bf16[448,2048]{1,0:T(8,128)(2,1)} async-done(((bf16[1792,2048]{1,0:T(8,128)(2,1)}), bf16[448,2048]{1,0:T(8,128)(2,1)}) %reduce-scatter.2.cloned.1.call-update) | async-done | bytes 1835024 | tf_op jit(solution)/shard_map/reduce_scatter | solution.py:168
  368.6 3.6 reshape.173
  372.3 7.9 %all-to-all-start.2 = ((bf16[32,14,2048]{2,1,0:T(8,128)(2,1)}), bf16[32,14,2048]{2,1,0:T(8,128)(2,1)}, u32[]{:S(2)}, u32[]{:S(2)}) async-start(bf16[32,14,2048]{2,1,0:T(8,128)(2,1)} %reshape.173), calls=%async_computation.3 | async-start | bytes 4194304 | tf_op jit(solution)/shard_map/all_to_all | solution.py:169
  380.7 11.3 %copy.91 = bf16[256,8,2,1408]{3,1,2,0:T(8,128)(2,1)} copy(bf16[256,8,2,1408]{3,2,1,0:T(2,128)(2,1)} %bitcast.103) | data formatting | bytes 23068672
  391.9 15.2 %copy.68 = bf16[2816,2048]{1,0:T(8,128)(2,1)} copy(bf16[2816,2048]{0,1:T(8,128)(2,1)} %bitcast.101) | data formatting | bytes 23068672 | tf_op jit(solution)/shard_map/dot_general | solution.py:153
  407.2 8.7 %fusion.25 = f32[64,2,1408]{2,0,1:T(8,128)} fusion(bf16[2,1408,2048]{2,1,0:T(8,128)(2,1)} %bitcast.100, bf16[64,2048]{1,0:T(8,128)(2,1)S(1)} %copy-done.7), kind=kOutput, calls=%fused_computation.52 | convolution fusion | flops 738197504 | bytes 12517376 | tf_op jit(solution)/shard_map/dot_general | solution.py:153
  418.5 3.1 gather_fusion.1
  421.6 3.7 gather.12
  425.3 4.2 multiply_reduce_fusion
  429.5 4.5 %fusion.18 = bf16[64,2048]{1,0:T(8,128)(2,1)} fusion(f32[64,2048]{1,0:T(8,128)S(1)} %multiply_reduce_fusion, bf16[1408,2048]{1,0:T(8,128)(2,1)} %param.23, f32[64,2,1408]{2,0,1:T(8,128)S(1)} %copy-done.5, f32[64,2048]{1,0:T(8,128)S(1)} %reshape.167, bf16[64,5120]{1,0:T(8,128)(2,1)} %bitcast.108), kind=kOutput, calls=%fused_computation.34 | convolution fusion | flops 370204672 | bytes 8060928 | tf_op jit(solution)/shard_map/dot_general | solution.py:157
  (127 shorter events, 83.9 us)
Async XLA Ops:
  6.5 278.2 %copy-start = (bf16[1,2,352,2048]{3,2,1,0:T(8,128)(2,1)S(1)}, bf16[1,2,352,2048]{3,2,1,0:T(8,128)(2,1)}, u32[]{:S(2)}) copy-start(bf16[1,2,352,2048]{3,2,1,0:T(8,128)(2,1)} %param.24) | copy-start | bytes 8650756
  6.5 68.5 %all-gather.2.cloned.1.call-start = ((), (), s32[]{:S(2)}) async-start(), calls=%async_computation.4 | async-start | bytes 4325376 | tf_op jit(solution)/shard_map/all_gather | solution.py:94
  26.1 48.9 %copy-start.4 = (bf16[4,16,5120]{2,1,0:T(8,128)(2,1)}, bf16[4,16,5120]{2,1,0:T(8,128)(2,1)S(1)}, u32[]{:S(2)}) copy-start(bf16[4,16,5120]{2,1,0:T(8,128)(2,1)S(1)} %all_to_all.15) | copy-start | bytes 1966084
  26.8 341.8 %reduce-scatter.2.cloned.1.call-start = ((), (), s32[]{:S(2)}) async-start(), calls=%async_computation.5 | async-start | bytes 9175040 | tf_op jit(solution)/shard_map/reduce_scatter | solution.py:168
  136.0 4.8 %copy-start.11 = (f32[2048]{0:T(1024)S(1)}, f32[2048]{0:T(1024)}, u32[]{:S(2)}) copy-start(f32[2048]{0:T(1024)} %param.21) | copy-start | bytes 24580
  137.3 5.3 %copy-start.8 = (pred[448,64]{0,1:T(8,128)(4,1)S(1)}, pred[448,64]{0,1:T(8,128)(4,1)}, u32[]{:S(2)}) copy-start(pred[448,64]{0,1:T(8,128)(4,1)} %fusion.22) | copy-start | bytes 86020
  141.9 0.7 copy-start.6
  181.6 1.4 copy-start.2
  185.2 43.0 %collective-permute-start = (bf16[32,14,2048]{2,0,1:T(8,128)(2,1)}, bf16[32,14,2048]{2,0,1:T(8,128)(2,1)}, u32[]{:S(2)}, u32[]{:S(2)}) collective-permute-start(bf16[32,14,2048]{2,0,1:T(8,128)(2,1)} %copy.74), channel_id=1, source_target_pairs={{0,32},{32,64},{64,96},{96,0},{1,33},{33,65},{65,97},{97,1},{2,34}... | collective-permute-start | bytes 5505032 | tf_op jit(solution)/shard_map/ppermute | solution.py:28
  186.4 51.4 %collective-permute-start.1 = (bf16[32,14,2048]{2,0,1:T(8,128)(2,1)}, bf16[32,14,2048]{2,0,1:T(8,128)(2,1)}, u32[]{:S(2)}, u32[]{:S(2)}) collective-permute-start(bf16[32,14,2048]{2,0,1:T(8,128)(2,1)} %copy.74), channel_id=1, source_target_pairs={{0,96},{32,0},{64,32},{96,64},{1,97},{33,1},{65,33},{97,65},{2,98}... | collective-permute-start | bytes 5505032 | tf_op jit(solution)/shard_map/ppermute | solution.py:35
  228.2 42.1 %collective-permute-start.2 = (bf16[32,14,2048]{2,0,1:T(8,128)(2,1)}, bf16[32,14,2048]{2,0,1:T(8,128)(2,1)}, u32[]{:S(2)}, u32[]{:S(2)}) collective-permute-start(bf16[32,14,2048]{2,0,1:T(8,128)(2,1)} %collective-permute-done), channel_id=1, source_target_pairs={{0,32},{32,64},{64,96},{96,0},{1,33},{33,65},{65,97},{97,1},{2,34}... | collective-permute-start | bytes 5505032 | tf_op jit(solution)/shard_map/ppermute | solution.py:28
  228.2 4.3 copy-start.3
  284.7 8.6 %copy-start.14 = (bf16[1,352,2048]{2,1,0:T(8,128)(2,1)S(1)}, bf16[1,352,2048]{2,1,0:T(8,128)(2,1)}, u32[]{:S(2)}) copy-start(bf16[1,352,2048]{2,1,0:T(8,128)(2,1)} %param.25) | copy-start | bytes 4325380
  372.2 8.0 %copy-start.9 = (s32[64,6]{0,1:T(8,128)S(1)}, s32[64,6]{0,1:T(8,128)}, u32[]{:S(2)}) copy-start(s32[64,6]{0,1:T(8,128)} %param.19) | copy-start | bytes 4612
  372.3 8.2 %copy-start.13 = (pred[64,6]{0,1:T(8,128)(4,1)S(1)}, pred[64,6]{0,1:T(8,128)(4,1)}, u32[]{:S(2)}) copy-start(pred[64,6]{0,1:T(8,128)(4,1)} %get-tuple-element.260) | copy-start | bytes 1156
  372.3 8.3 %copy-start.12 = (f32[64,6]{0,1:T(8,128)S(1)}, f32[64,6]{0,1:T(8,128)}, u32[]{:S(2)}) copy-start(f32[64,6]{0,1:T(8,128)} %param.20) | copy-start | bytes 4612
  372.3 43.7 %all-to-all-start.2 = ((bf16[32,14,2048]{2,1,0:T(8,128)(2,1)}), bf16[32,14,2048]{2,1,0:T(8,128)(2,1)}, u32[]{:S(2)}, u32[]{:S(2)}) async-start(bf16[32,14,2048]{2,1,0:T(8,128)(2,1)} %reshape.173), calls=%async_computation.3 | async-start | bytes 4194304 | tf_op jit(solution)/shard_map/all_to_all | solution.py:169
  391.9 15.2 %copy-start.10 = (s32[384]{0:T(512)S(1)}, s32[384]{0:T(512)}, u32[]{:S(2)}) copy-start(s32[384]{0:T(512)} %fusion.30) | copy-start | bytes 4612
  391.9 15.2 %copy-start.7 = (bf16[64,2048]{1,0:T(8,128)(2,1)S(1)}, bf16[64,2048]{1,0:T(8,128)(2,1)}, u32[]{:S(2)}) copy-start(bf16[64,2048]{1,0:T(8,128)(2,1)} %copy-done.6) | copy-start | bytes 786436
  425.3 4.2 copy-start.5
  425.3 8.7 %copy-start.1 = (bf16[1,2,352,2048]{3,2,1,0:T(8,128)(2,1)S(1)}, bf16[1,2,352,2048]{3,2,1,0:T(8,128)(2,1)}, u32[]{:S(2)}) copy-start(bf16[1,2,352,2048]{3,2,1,0:T(8,128)(2,1)} %param.24) | copy-start | bytes 8650756
Sparse Core Ops, SparseCore 0:
  26.9 48.0 all-gather.1
  299.6 68.9 reduce-scatter.1
